TPU v7x, 32 devices: a whole 2x2x4 slice. The times are simulated.
32 devices in a mesh: groups: 2 (over x), seq: 4 (over y, core), pair: 4 (over z).
Axes of the slice: x: 2, y: 2, z: 4, core: 2. Of those that a mesh axis runs over, the one named last changes fastest.
Arguments:
- sequence: bfloat16 [4096, 1536], P(('groups', 'seq', 'pair')), parts along dimension 0, may hold values from -12 to 12
- gain_conv: float32 [1536], replicated, may hold values from 0.25 to 1.75
- conv_weight: bfloat16 [5, 1536, 1536], P(None, 'pair'), may hold values from -0.0625 to 0.0625
- gain_attn: float32 [1536], replicated, may hold values from 0.25 to 1.75
- w_qkv: bfloat16 [1536, 3072], P(None, 'pair'), may hold values from -1 to 1
- w_out: bfloat16 [1024, 1536], P('pair'), may hold values from -0.75 to 0.75
- gain_pool: float32 [1536], replicated, may hold values from 0.25 to 1.75
- w_pair: bfloat16 [1536, 256], replicated, may hold values from -0.15625 to 0.15625
- w_up: bfloat16 [128, 256], replicated, may hold values from -0.5 to 0.5
- w_down: bfloat16 [256, 128], replicated, may hold values from -0.375 to 0.375
Outputs:
- seq_out: bfloat16 [4096, 1536], P(('groups', 'seq', 'pair')), parts along dimension 0
- pair_map: bfloat16 [256, 128, 128], P(('groups', 'seq'), 'pair'), parts along dimension 0
There are 2 independent parts, one for each index of `groups`. A program takes and returns all parts, laid end to end along the dimension named above; an argument that names none is the same for every part. Nothing has to cross between parts.
All inputs are finite; a program needn't handle non-finite values.
Results may differ from a plain program's by a relative error of at most 0.024.
Values may be sent and summed in bfloat16 or wider, within the bound.
No kernel may reach another device: no remote copies, remote signals or barrier semaphores. Data moves between devices by JAX's collectives and lax.ppermute only.
A program may use at most 64 MiB of HBM per device.

v0:
```python
import math
import jax
import jax.numpy as jnp
from jax import lax
from jax.sharding import PartitionSpec as P

KEY_SIZE = 128
VALUE_SIZE = 128
DILATION = 4
POOL = 16
PAIR_CH = 128
EPS = 1e-06


def padded_2(value, sides, width):
    for axis, dim in sides:
        peers, length = (lax.axis_size(axis), value.shape[dim])
        up = [(i, (i + 1) % peers) for i in range(peers - 1)]
        down = [(j, i) for i, j in up]
        last = lax.slice_in_dim(value, length - width, length, axis=dim)
        first = lax.slice_in_dim(value, 0, width, axis=dim)
        before = lax.ppermute(last, axis, up)
        after = lax.ppermute(first, axis, down)
        value = jnp.concatenate([before, value, after], axis=dim)
    return value


def norm_rows(values, gain):
    return values * lax.rsqrt(jnp.mean(values * values, axis=-1, keepdims=True) + EPS) * gain


def conv_rows(padded, conv_weight, row_total):
    summed = jnp.zeros((row_total, conv_weight.shape[2]), jnp.float32)
    for offset in range(conv_weight.shape[0]):
        shifted = lax.dynamic_slice_in_dim(padded, offset * DILATION, row_total, 0)
        summed = summed + jnp.dot(shifted, conv_weight[offset], preferred_element_type=jnp.float32)
    return summed


def line_reduce_scatter(partial, axis):
    n = lax.axis_size(axis)
    me = lax.axis_index(axis)
    rows = partial.shape[0] // n
    blocks = partial.reshape(n, rows, partial.shape[1])
    right = [(i, i + 1) for i in range(n - 1)]
    left = [(i + 1, i) for i in range(n - 1)]
    got_r = jnp.zeros((rows, partial.shape[1]), jnp.bfloat16)
    got_l = jnp.zeros((rows, partial.shape[1]), jnp.bfloat16)
    for step in range(1, n):
        idx_r = jnp.clip(me + n - step, 0, n - 1)
        idx_l = jnp.clip(me - (n - step), 0, n - 1)
        send_r = (blocks[idx_r] + got_r.astype(jnp.float32)).astype(jnp.bfloat16)
        send_l = (blocks[idx_l] + got_l.astype(jnp.float32)).astype(jnp.bfloat16)
        got_r = lax.ppermute(send_r, axis, right)
        got_l = lax.ppermute(send_l, axis, left)
    own = blocks[me]
    return own + got_r.astype(jnp.float32) + got_l.astype(jnp.float32)


def line_all_gather(value, axis):
    n = lax.axis_size(axis)
    me = lax.axis_index(axis)
    rows = value.shape[0]
    right = [(i, i + 1) for i in range(n - 1)]
    left = [(i + 1, i) for i in range(n - 1)]
    slots = jnp.zeros((n + 1, rows) + value.shape[1:], value.dtype)
    slots = lax.dynamic_update_index_in_dim(slots, value, me, 0)
    flow_r, flow_l = (value, value)
    for step in range(1, n):
        flow_r = lax.ppermute(flow_r, axis, right)
        flow_l = lax.ppermute(flow_l, axis, left)
        at_r = jnp.where(me - step >= 0, me - step, n)
        at_l = jnp.where(me + step < n, me + step, n)
        slots = lax.dynamic_update_index_in_dim(slots, flow_r, at_r, 0)
        slots = lax.dynamic_update_index_in_dim(slots, flow_l, at_l, 0)
    return slots[:n].reshape((n * rows,) + value.shape[1:])


def doubling_all_gather(value, axis):
    n = lax.axis_size(axis)
    assert n & n - 1 == 0
    me = lax.axis_index(axis)
    out = value
    k = 1
    while k < n:
        other = lax.ppermute(out, axis, [(i, i ^ k) for i in range(n)])
        low = me & k == 0
        out = jnp.where(low, jnp.concatenate([out, other], 0), jnp.concatenate([other, out], 0))
        k *= 2
    return out


def shards(
    sequence, gain_conv, conv_weight, gain_attn, w_qkv, w_out, gain_pool, w_pair, w_up, w_down
):
    pair_count = lax.axis_size("pair")
    seq_count = lax.axis_size("seq")
    row_count = sequence.shape[0]
    channels = sequence.shape[1]
    local_rows = row_count * pair_count
    inputs = sequence.astype(jnp.float32)
    normed = norm_rows(inputs, gain_conv).astype(jnp.bfloat16)
    swapped = lax.all_to_all(normed, "pair", split_axis=1, concat_axis=0, tiled=True)
    padded = padded_2(swapped, (("seq", 0),), DILATION * (conv_weight.shape[0] - 1) // 2)
    with jax.named_scope("conv_reduce"):
        summed = line_reduce_scatter(conv_rows(padded, conv_weight, local_rows), "pair")
    first_out = (inputs + summed).astype(jnp.bfloat16)
    attn_in = norm_rows(first_out.astype(jnp.float32), gain_attn).astype(jnp.bfloat16)
    with jax.named_scope("attn_in_gather"):
        block_in = line_all_gather(attn_in, "pair")
    projected = jnp.dot(block_in, w_qkv, preferred_element_type=jnp.float32).astype(jnp.bfloat16)
    head_count = projected.shape[1] // (2 * KEY_SIZE + VALUE_SIZE)
    grouped = projected.reshape(local_rows, head_count, 2 * KEY_SIZE + VALUE_SIZE).transpose(
        1, 0, 2
    )
    queries = grouped[:, :, :KEY_SIZE]
    kv = grouped[:, :, KEY_SIZE:]
    scale = 1.0 / math.sqrt(KEY_SIZE)
    ring = [(i, (i + 1) % seq_count) for i in range(seq_count)]

    def attend(state, kv_block):
        running_max, running_sum, weighted = state
        key_block = kv_block[:, :, :KEY_SIZE]
        value_block = kv_block[:, :, KEY_SIZE:]
        scores = (
            jnp.einsum("hqd,hkd->hqk", queries, key_block, preferred_element_type=jnp.float32)
            * scale
        )
        new_max = jnp.maximum(running_max, jnp.max(scores, axis=-1))
        shrink = jnp.exp(running_max - new_max)
        weights = jnp.exp(scores - new_max[:, :, None])
        running_sum = running_sum * shrink + jnp.sum(weights, axis=-1)
        update = jnp.einsum(
            "hqk,hkd->hqd",
            weights.astype(jnp.bfloat16),
            value_block,
            preferred_element_type=jnp.float32,
        )
        weighted = weighted * shrink[:, :, None] + update
        return (new_max, running_sum, weighted)

    state = (
        jnp.full((head_count, local_rows), -1e30, jnp.float32),
        jnp.zeros((head_count, local_rows), jnp.float32),
        jnp.zeros((head_count, local_rows, VALUE_SIZE), jnp.float32),
    )
    with jax.named_scope("kv_ring"):
        current = kv
        for step in range(seq_count):
            if step + 1 < seq_count:
                arriving = lax.ppermute(current, "seq", ring)
            state = attend(state, current)
            if step + 1 < seq_count:
                current = arriving
    running_max, running_sum, weighted = state
    attended = (weighted / running_sum[:, :, None]).astype(jnp.bfloat16)
    attended = attended.transpose(1, 0, 2).reshape(local_rows, head_count * VALUE_SIZE)
    with jax.named_scope("out_reduce"):
        mixed = line_reduce_scatter(
            jnp.dot(attended, w_out, preferred_element_type=jnp.float32), "pair"
        )
    seq_out = (first_out.astype(jnp.float32) + mixed).astype(jnp.bfloat16)
    bin_count = row_count // POOL
    pooled = jnp.mean(seq_out.astype(jnp.float32).reshape(bin_count, POOL, channels), axis=1)
    bin_norm = norm_rows(pooled, gain_pool).astype(jnp.bfloat16)
    sides = jnp.dot(bin_norm, w_pair, preferred_element_type=jnp.float32).astype(jnp.bfloat16)
    with jax.named_scope("sides_gather"):
        all_sides = doubling_all_gather(doubling_all_gather(sides, "pair"), "seq")
    tile_rows = bin_count * pair_count
    tile_cols = bin_count * seq_count
    row_side = lax.dynamic_slice_in_dim(all_sides, lax.axis_index("seq") * tile_rows, tile_rows, 0)[
        :, :PAIR_CH
    ]
    column_side = lax.dynamic_slice_in_dim(
        all_sides, lax.axis_index("pair") * tile_cols, tile_cols, 0
    )[:, PAIR_CH:]
    pair_tile = (
        row_side.astype(jnp.float32)[:, None, :] * column_side.astype(jnp.float32)[None, :, :]
    ).astype(jnp.bfloat16)
    flat_rows = pair_tile.reshape(tile_rows * tile_cols, PAIR_CH)
    hidden = jax.nn.relu(jnp.dot(flat_rows, w_up, preferred_element_type=jnp.float32)).astype(
        jnp.bfloat16
    )
    pair_out = flat_rows.astype(jnp.float32) + jnp.dot(
        hidden, w_down, preferred_element_type=jnp.float32
    )
    pair_map = pair_out.astype(jnp.bfloat16).reshape(tile_rows, tile_cols, PAIR_CH)
    return (seq_out, pair_map)


def solution(mesh):
    return jax.shard_map(
        shards,
        mesh=mesh,
        in_specs=(
            P(("groups", "seq", "pair"), None),
            P(),
            P(None, "pair", None),
            P(),
            P(None, "pair"),
            P("pair", None),
            P(),
            P(),
            P(),
            P(),
        ),
        out_specs=(P(("groups", "seq", "pair"), None), P(("groups", "seq"), "pair", None)),
        check_vma=False,
    )
```

profile of v0, /device:TPU:0, one launch (start us, length us, event | category | flops | bytes accessed | tf_op | source)
XLA Modules:
  0.0 228.1 jit_solution(8391843378703551363)
XLA Ops:
  3.9 6.3 %all-to-all-start = ((bf16[128,4,384]{2,0,1:T(8,128)(2,1)}), bf16[128,4,384]{2,0,1:T(8,128)(2,1)S(1)}, u32[]{:S(2)}, u32[]{:S(2)}) async-start(bf16[128,4,384]{2,0,1:T(8,128)(2,1)} %bitcast.205), calls=%async_computation | async-start | bytes 786432 | tf_op jit(solution)/shard_map/all_to_all | solution.py:103
  10.2 11.7 %all-to-all-done = bf16[128,4,384]{2,0,1:T(8,128)(2,1)S(1)} async-done(((bf16[128,4,384]{2,0,1:T(8,128)(2,1)}), bf16[128,4,384]{2,0,1:T(8,128)(2,1)S(1)}, u32[]{:S(2)}, u32[]{:S(2)}) %all-to-all-start) | async-done | bytes 393248 | tf_op jit(solution)/shard_map/all_to_all | solution.py:103
  38.7 5.8 %collective-permute-done.2 = bf16[128,1536]{1,0:T(8,128)(2,1)} collective-permute-done((bf16[128,1536]{1,0:T(8,128)(2,1)S(1)}, bf16[128,1536]{1,0:T(8,128)(2,1)}, u32[]{:S(2)}, u32[]{:S(2)}) %collective-permute-start.2) | collective-permute-done | bytes 393248 | tf_op jit(solution)/shard_map/conv_reduce/ppermute | solution.py:54
  45.8 5.2 %collective-permute-start.3 = (bf16[128,1536]{1,0:T(8,128)(2,1)S(1)}, bf16[128,1536]{1,0:T(8,128)(2,1)}, u32[]{:S(2)}, u32[]{:S(2)}) collective-permute-start(bf16[128,1536]{1,0:T(8,128)(2,1)S(1)} %fusion.65), channel_id=1, source_target_pairs={{0,1},{1,2},{2,3},{4,5},{5,6},{6,7},{8,9},{9,10},{10,11},{12,13},{... | collective-permute-start | bytes 1179656 | tf_op jit(solution)/shard_map/conv_reduce/ppermute | solution.py:54
  51.1 8.0 %collective-permute-done.3 = bf16[128,1536]{1,0:T(8,128)(2,1)} collective-permute-done((bf16[128,1536]{1,0:T(8,128)(2,1)S(1)}, bf16[128,1536]{1,0:T(8,128)(2,1)}, u32[]{:S(2)}, u32[]{:S(2)}) %collective-permute-start.3) | collective-permute-done | bytes 393248 | tf_op jit(solution)/shard_map/conv_reduce/ppermute | solution.py:54
  62.9 5.9 %collective-permute-start.4 = (bf16[128,1536]{1,0:T(8,128)(2,1)}, bf16[128,1536]{1,0:T(8,128)(2,1)}, u32[]{:S(2)}, u32[]{:S(2)}) collective-permute-start(bf16[128,1536]{1,0:T(8,128)(2,1)} %get-tuple-element.18), channel_id=1, source_target_pairs={{0,1},{1,2},{2,3},{4,5},{5,6},{6,7},{8,9},{9,10},{10,11},{12,13},{... | collective-permute-start | bytes 1179656 | tf_op jit(solution)/shard_map/conv_reduce/ppermute | solution.py:54
  68.8 7.1 %collective-permute-done.6 = bf16[128,1536]{1,0:T(8,128)(2,1)S(1)} collective-permute-done((bf16[128,1536]{1,0:T(8,128)(2,1)S(1)}, bf16[128,1536]{1,0:T(8,128)(2,1)S(1)}, u32[]{:S(2)}, u32[]{:S(2)}) %collective-permute-start.6) | collective-permute-done | bytes 393248 | tf_op jit(solution)/shard_map/conv_reduce/ppermute | solution.py:55
  78.4 11.6 %collective-permute-done.7 = bf16[128,1536]{1,0:T(8,128)(2,1)S(1)} collective-permute-done((bf16[128,1536]{1,0:T(8,128)(2,1)S(1)}, bf16[128,1536]{1,0:T(8,128)(2,1)S(1)}, u32[]{:S(2)}, u32[]{:S(2)}) %collective-permute-start.7) | collective-permute-done | bytes 393248 | tf_op jit(solution)/shard_map/conv_reduce/ppermute | solution.py:55
  94.1 3.6 %collective-permute-start.8 = (bf16[128,1536]{1,0:T(8,128)(2,1)}, bf16[128,1536]{1,0:T(8,128)(2,1)S(1)}, u32[]{:S(2)}, u32[]{:S(2)}) collective-permute-start(bf16[128,1536]{1,0:T(8,128)(2,1)} %get-tuple-element.11), channel_id=1, source_target_pairs={{0,1},{1,2},{2,3},{4,5},{5,6},{6,7},{8,9},{9,10},{10,11},{12,13},{... | collective-permute-start | bytes 1179656 | tf_op jit(solution)/shard_map/attn_in_gather/ppermute | solution.py:70
  99.0 6.5 %collective-permute-done.8 = bf16[128,1536]{1,0:T(8,128)(2,1)S(1)} collective-permute-done((bf16[128,1536]{1,0:T(8,128)(2,1)}, bf16[128,1536]{1,0:T(8,128)(2,1)S(1)}, u32[]{:S(2)}, u32[]{:S(2)}) %collective-permute-start.8) | collective-permute-done | bytes 393248 | tf_op jit(solution)/shard_map/attn_in_gather/ppermute | solution.py:70
  105.5 4.3 %collective-permute-start.10 = (bf16[128,1536]{1,0:T(8,128)(2,1)S(1)}, bf16[128,1536]{1,0:T(8,128)(2,1)S(1)}, u32[]{:S(2)}, u32[]{:S(2)}) collective-permute-start(bf16[128,1536]{1,0:T(8,128)(2,1)S(1)} %collective-permute-done.8), channel_id=1, source_target_pairs={{0,1},{1,2},{2,3},{4,5},{5,6},{6,7},{8,9},{9,10},{10,11},{12,13},{... | collective-permute-start | bytes 1179656 | tf_op jit(solution)/shard_map/attn_in_gather/ppermute | solution.py:70
  112.7 3.8 %collective-permute-done.10 = bf16[128,1536]{1,0:T(8,128)(2,1)S(1)} collective-permute-done((bf16[128,1536]{1,0:T(8,128)(2,1)S(1)}, bf16[128,1536]{1,0:T(8,128)(2,1)S(1)}, u32[]{:S(2)}, u32[]{:S(2)}) %collective-permute-start.10) | collective-permute-done | bytes 393248 | tf_op jit(solution)/shard_map/attn_in_gather/ppermute | solution.py:70
  116.5 4.4 %collective-permute-start.12 = (bf16[128,1536]{1,0:T(8,128)(2,1)S(1)}, bf16[128,1536]{1,0:T(8,128)(2,1)S(1)}, u32[]{:S(2)}, u32[]{:S(2)}) collective-permute-start(bf16[128,1536]{1,0:T(8,128)(2,1)S(1)} %collective-permute-done.10), channel_id=1, source_target_pairs={{0,1},{1,2},{2,3},{4,5},{5,6},{6,7},{8,9},{9,10},{10,11},{12,13},{... | collective-permute-start | bytes 1179656 | tf_op jit(solution)/shard_map/attn_in_gather/ppermute | solution.py:70
  127.4 3.4 %collective-permute-done.13 = bf16[128,1536]{1,0:T(8,128)(2,1)S(1)} collective-permute-done((bf16[128,1536]{1,0:T(8,128)(2,1)S(1)}, bf16[128,1536]{1,0:T(8,128)(2,1)S(1)}, u32[]{:S(2)}, u32[]{:S(2)}) %collective-permute-start.13) | collective-permute-done | bytes 393248 | tf_op jit(solution)/shard_map/attn_in_gather/ppermute | solution.py:71
  134.6 8.6 %collective-permute-done.14 = bf16[2,512,256]{2,1,0:T(8,128)(2,1)S(1)} collective-permute-done((bf16[2,512,256]{2,1,0:T(8,128)(2,1)S(1)}, bf16[2,512,256]{2,1,0:T(8,128)(2,1)S(1)}, u32[]{:S(2)}, u32[]{:S(2)}) %collective-permute-start.14) | collective-permute-done | bytes 524320 | tf_op jit(solution)/shard_map/kv_ring/ppermute | solution.py:151
  143.7 8.2 %collective-permute-done.15 = bf16[2,512,256]{2,1,0:T(8,128)(2,1)S(1)} collective-permute-done((bf16[2,512,256]{2,1,0:T(8,128)(2,1)S(1)}, bf16[2,512,256]{2,1,0:T(8,128)(2,1)S(1)}, u32[]{:S(2)}, u32[]{:S(2)}) %collective-permute-start.15) | collective-permute-done | bytes 524320 | tf_op jit(solution)/shard_map/kv_ring/ppermute | solution.py:151
  152.7 7.7 %collective-permute-done.16 = bf16[2,512,256]{2,1,0:T(8,128)(2,1)S(1)} collective-permute-done((bf16[2,512,256]{2,1,0:T(8,128)(2,1)S(1)}, bf16[2,512,256]{2,1,0:T(8,128)(2,1)S(1)}, u32[]{:S(2)}, u32[]{:S(2)}) %collective-permute-start.16) | collective-permute-done | bytes 524320 | tf_op jit(solution)/shard_map/kv_ring/ppermute | solution.py:151
  171.1 7.1 %collective-permute-done.17 = bf16[128,1536]{1,0:T(8,128)(2,1)S(1)} collective-permute-done((bf16[128,1536]{1,0:T(8,128)(2,1)S(1)}, bf16[128,1536]{1,0:T(8,128)(2,1)S(1)}, u32[]{:S(2)}, u32[]{:S(2)}) %collective-permute-start.17) | collective-permute-done | bytes 393248 | tf_op jit(solution)/shard_map/out_reduce/ppermute | solution.py:54
  178.2 4.4 %collective-permute-start.18 = (bf16[128,1536]{1,0:T(8,128)(2,1)S(1)}, bf16[128,1536]{1,0:T(8,128)(2,1)S(1)}, u32[]{:S(2)}, u32[]{:S(2)}) collective-permute-start(bf16[128,1536]{1,0:T(8,128)(2,1)S(1)} %fusion.58), channel_id=1, source_target_pairs={{0,1},{1,2},{2,3},{4,5},{5,6},{6,7},{8,9},{9,10},{10,11},{12,13},{... | collective-permute-start | bytes 1179656 | tf_op jit(solution)/shard_map/out_reduce/ppermute | solution.py:54
  182.7 7.3 %collective-permute-done.18 = bf16[128,1536]{1,0:T(8,128)(2,1)S(1)} collective-permute-done((bf16[128,1536]{1,0:T(8,128)(2,1)S(1)}, bf16[128,1536]{1,0:T(8,128)(2,1)S(1)}, u32[]{:S(2)}, u32[]{:S(2)}) %collective-permute-start.18) | collective-permute-done | bytes 393248 | tf_op jit(solution)/shard_map/out_reduce/ppermute | solution.py:54
  191.6 5.0 %collective-permute-start.19 = (bf16[128,1536]{1,0:T(8,128)(2,1)S(1)}, bf16[128,1536]{1,0:T(8,128)(2,1)S(1)}, u32[]{:S(2)}, u32[]{:S(2)}) collective-permute-start(bf16[128,1536]{1,0:T(8,128)(2,1)S(1)} %get-tuple-element.14), channel_id=1, source_target_pairs={{0,1},{1,2},{2,3},{4,5},{5,6},{6,7},{8,9},{9,10},{10,11},{12,13},{... | collective-permute-start | bytes 1179656 | tf_op jit(solution)/shard_map/out_reduce/ppermute | solution.py:54
  196.6 5.5 %collective-permute-done.21 = bf16[128,1536]{1,0:T(8,128)(2,1)S(1)} collective-permute-done((bf16[128,1536]{1,0:T(8,128)(2,1)S(1)}, bf16[128,1536]{1,0:T(8,128)(2,1)S(1)}, u32[]{:S(2)}, u32[]{:S(2)}) %collective-permute-start.21) | collective-permute-done | bytes 393248 | tf_op jit(solution)/shard_map/out_reduce/ppermute | solution.py:55
  203.7 8.4 %collective-permute-done.22 = bf16[128,1536]{1,0:T(8,128)(2,1)S(1)} collective-permute-done((bf16[128,1536]{1,0:T(8,128)(2,1)S(1)}, bf16[128,1536]{1,0:T(8,128)(2,1)S(1)}, u32[]{:S(2)}, u32[]{:S(2)}) %collective-permute-start.22) | collective-permute-done | bytes 393248 | tf_op jit(solution)/shard_map/out_reduce/ppermute | solution.py:55
  222.9 3.9 %collective-permute-done.26 = bf16[64,256]{1,0:T(8,128)(2,1)S(1)} collective-permute-done((bf16[64,256]{1,0:T(8,128)(2,1)S(1)}, bf16[64,256]{1,0:T(8,128)(2,1)S(1)}, u32[]{:S(2)}, u32[]{:S(2)}) %collective-permute-start.26) | collective-permute-done | bytes 32800 | tf_op jit(solution)/shard_map/sides_gather/ppermute | solution.py:86
  (108 shorter events, 73.4 us)
Async XLA Ops:
  3.9 18.0 %all-to-all-start = ((bf16[128,4,384]{2,0,1:T(8,128)(2,1)}), bf16[128,4,384]{2,0,1:T(8,128)(2,1)S(1)}, u32[]{:S(2)}, u32[]{:S(2)}) async-start(bf16[128,4,384]{2,0,1:T(8,128)(2,1)} %bitcast.205), calls=%async_computation | async-start | bytes 786432 | tf_op jit(solution)/shard_map/all_to_all | solution.py:103
  21.9 5.3 %collective-permute-start = (bf16[8,384]{1,0:T(8,128)(2,1)S(1)}, bf16[8,384]{1,0:T(8,128)(2,1)S(1)}, u32[]{:S(2)}, u32[]{:S(2)}) collective-permute-start(bf16[8,384]{1,0:T(8,128)(2,1)S(1)} %get-tuple-element.22), channel_id=1, source_target_pairs={{0,4},{4,8},{8,12},{1,5},{5,9},{9,13},{2,6},{6,10},{10,14},{3,7},{... | collective-permute-start | bytes 18440 | tf_op jit(solution)/shard_map/ppermute | solution.py:22
  25.9 4.6 %collective-permute-start.1 = (bf16[8,384]{1,0:T(8,128)(2,1)S(1)}, bf16[8,384]{1,0:T(8,128)(2,1)S(1)}, u32[]{:S(2)}, u32[]{:S(2)}) collective-permute-start(bf16[8,384]{1,0:T(8,128)(2,1)S(1)} %get-tuple-element.23), channel_id=1, source_target_pairs={{4,0},{8,4},{12,8},{5,1},{9,5},{13,9},{6,2},{10,6},{14,10},{7,3},{... | collective-permute-start | bytes 18440 | tf_op jit(solution)/shard_map/ppermute | solution.py:23
  35.2 9.3 %collective-permute-start.2 = (bf16[128,1536]{1,0:T(8,128)(2,1)S(1)}, bf16[128,1536]{1,0:T(8,128)(2,1)}, u32[]{:S(2)}, u32[]{:S(2)}) collective-permute-start(bf16[128,1536]{1,0:T(8,128)(2,1)S(1)} %get-tuple-element.20), channel_id=1, source_target_pairs={{0,1},{1,2},{2,3},{4,5},{5,6},{6,7},{8,9},{9,10},{10,11},{12,13},{... | collective-permute-start | bytes 1179656 | tf_op jit(solution)/shard_map/conv_reduce/ppermute | solution.py:54
  37.4 13.7 %collective-permute-start.5 = (bf16[128,1536]{1,0:T(8,128)(2,1)S(1)}, bf16[128,1536]{1,0:T(8,128)(2,1)}, u32[]{:S(2)}, u32[]{:S(2)}) collective-permute-start(bf16[128,1536]{1,0:T(8,128)(2,1)S(1)} %get-tuple-element.21), channel_id=1, source_target_pairs={{1,0},{2,1},{3,2},{5,4},{6,5},{7,6},{9,8},{10,9},{11,10},{13,12},{... | collective-permute-start | bytes 1179656 | tf_op jit(solution)/shard_map/conv_reduce/ppermute | solution.py:55
  45.8 13.2 %collective-permute-start.3 = (bf16[128,1536]{1,0:T(8,128)(2,1)S(1)}, bf16[128,1536]{1,0:T(8,128)(2,1)}, u32[]{:S(2)}, u32[]{:S(2)}) collective-permute-start(bf16[128,1536]{1,0:T(8,128)(2,1)S(1)} %fusion.65), channel_id=1, source_target_pairs={{0,1},{1,2},{2,3},{4,5},{5,6},{6,7},{8,9},{9,10},{10,11},{12,13},{... | collective-permute-start | bytes 1179656 | tf_op jit(solution)/shard_map/conv_reduce/ppermute | solution.py:54
  61.6 14.3 %collective-permute-start.6 = (bf16[128,1536]{1,0:T(8,128)(2,1)S(1)}, bf16[128,1536]{1,0:T(8,128)(2,1)S(1)}, u32[]{:S(2)}, u32[]{:S(2)}) collective-permute-start(bf16[128,1536]{1,0:T(8,128)(2,1)S(1)} %get-tuple-element.19), channel_id=1, source_target_pairs={{1,0},{2,1},{3,2},{5,4},{6,5},{7,6},{9,8},{10,9},{11,10},{13,12},{... | collective-permute-start | bytes 1179656 | tf_op jit(solution)/shard_map/conv_reduce/ppermute | solution.py:55
  62.9 15.6 %collective-permute-start.4 = (bf16[128,1536]{1,0:T(8,128)(2,1)}, bf16[128,1536]{1,0:T(8,128)(2,1)}, u32[]{:S(2)}, u32[]{:S(2)}) collective-permute-start(bf16[128,1536]{1,0:T(8,128)(2,1)} %get-tuple-element.18), channel_id=1, source_target_pairs={{0,1},{1,2},{2,3},{4,5},{5,6},{6,7},{8,9},{9,10},{10,11},{12,13},{... | collective-permute-start | bytes 1179656 | tf_op jit(solution)/shard_map/conv_reduce/ppermute | solution.py:54
  77.1 12.9 %collective-permute-start.7 = (bf16[128,1536]{1,0:T(8,128)(2,1)S(1)}, bf16[128,1536]{1,0:T(8,128)(2,1)S(1)}, u32[]{:S(2)}, u32[]{:S(2)}) collective-permute-start(bf16[128,1536]{1,0:T(8,128)(2,1)S(1)} %fusion.64), channel_id=1, source_target_pairs={{1,0},{2,1},{3,2},{5,4},{6,5},{7,6},{9,8},{10,9},{11,10},{13,12},{... | collective-permute-start | bytes 1179656 | tf_op jit(solution)/shard_map/conv_reduce/ppermute | solution.py:55
  94.1 11.4 %collective-permute-start.8 = (bf16[128,1536]{1,0:T(8,128)(2,1)}, bf16[128,1536]{1,0:T(8,128)(2,1)S(1)}, u32[]{:S(2)}, u32[]{:S(2)}) collective-permute-start(bf16[128,1536]{1,0:T(8,128)(2,1)} %get-tuple-element.11), channel_id=1, source_target_pairs={{0,1},{1,2},{2,3},{4,5},{5,6},{6,7},{8,9},{9,10},{10,11},{12,13},{... | collective-permute-start | bytes 1179656 | tf_op jit(solution)/shard_map/attn_in_gather/ppermute | solution.py:70
  97.7 12.2 %collective-permute-start.9 = (bf16[128,1536]{1,0:T(8,128)(2,1)}, bf16[128,1536]{1,0:T(8,128)(2,1)S(1)}, u32[]{:S(2)}, u32[]{:S(2)}) collective-permute-start(bf16[128,1536]{1,0:T(8,128)(2,1)} %get-tuple-element.11), channel_id=1, source_target_pairs={{1,0},{2,1},{3,2},{5,4},{6,5},{7,6},{9,8},{10,9},{11,10},{13,12},{... | collective-permute-start | bytes 1179656 | tf_op jit(solution)/shard_map/attn_in_gather/ppermute | solution.py:71
  105.5 10.9 %collective-permute-start.10 = (bf16[128,1536]{1,0:T(8,128)(2,1)S(1)}, bf16[128,1536]{1,0:T(8,128)(2,1)S(1)}, u32[]{:S(2)}, u32[]{:S(2)}) collective-permute-start(bf16[128,1536]{1,0:T(8,128)(2,1)S(1)} %collective-permute-done.8), channel_id=1, source_target_pairs={{0,1},{1,2},{2,3},{4,5},{5,6},{6,7},{8,9},{9,10},{10,11},{12,13},{... | collective-permute-start | bytes 1179656 | tf_op jit(solution)/shard_map/attn_in_gather/ppermute | solution.py:70
  109.9 11.0 %collective-permute-start.11 = (bf16[128,1536]{1,0:T(8,128)(2,1)S(1)}, bf16[128,1536]{1,0:T(8,128)(2,1)S(1)}, u32[]{:S(2)}, u32[]{:S(2)}) collective-permute-start(bf16[128,1536]{1,0:T(8,128)(2,1)S(1)} %collective-permute-done.9), channel_id=1, source_target_pairs={{1,0},{2,1},{3,2},{5,4},{6,5},{7,6},{9,8},{10,9},{11,10},{13,12},{... | collective-permute-start | bytes 1179656 | tf_op jit(solution)/shard_map/attn_in_gather/ppermute | solution.py:71
  116.5 10.1 %collective-permute-start.12 = (bf16[128,1536]{1,0:T(8,128)(2,1)S(1)}, bf16[128,1536]{1,0:T(8,128)(2,1)S(1)}, u32[]{:S(2)}, u32[]{:S(2)}) collective-permute-start(bf16[128,1536]{1,0:T(8,128)(2,1)S(1)} %collective-permute-done.10), channel_id=1, source_target_pairs={{0,1},{1,2},{2,3},{4,5},{5,6},{6,7},{8,9},{9,10},{10,11},{12,13},{... | collective-permute-start | bytes 1179656 | tf_op jit(solution)/shard_map/attn_in_gather/ppermute | solution.py:70
  120.9 9.8 %collective-permute-start.13 = (bf16[128,1536]{1,0:T(8,128)(2,1)S(1)}, bf16[128,1536]{1,0:T(8,128)(2,1)S(1)}, u32[]{:S(2)}, u32[]{:S(2)}) collective-permute-start(bf16[128,1536]{1,0:T(8,128)(2,1)S(1)} %collective-permute-done.11), channel_id=1, source_target_pairs={{1,0},{2,1},{3,2},{5,4},{6,5},{7,6},{9,8},{10,9},{11,10},{13,12},{... | collective-permute-start | bytes 1179656 | tf_op jit(solution)/shard_map/attn_in_gather/ppermute | solution.py:71
  134.6 8.7 %collective-permute-start.14 = (bf16[2,512,256]{2,1,0:T(8,128)(2,1)S(1)}, bf16[2,512,256]{2,1,0:T(8,128)(2,1)S(1)}, u32[]{:S(2)}, u32[]{:S(2)}) collective-permute-start(bf16[2,512,256]{2,1,0:T(8,128)(2,1)S(1)} %slice.92), channel_id=1, source_target_pairs={{0,4},{4,8},{8,12},{12,0},{1,5},{5,9},{9,13},{13,1},{2,6},{6,10},{... | collective-permute-start | bytes 1572872 | tf_op jit(solution)/shard_map/kv_ring/ppermute | solution.py:151
  143.2 8.6 %collective-permute-start.15 = (bf16[2,512,256]{2,1,0:T(8,128)(2,1)S(1)}, bf16[2,512,256]{2,1,0:T(8,128)(2,1)S(1)}, u32[]{:S(2)}, u32[]{:S(2)}) collective-permute-start(bf16[2,512,256]{2,1,0:T(8,128)(2,1)S(1)} %collective-permute-done.14), channel_id=1, source_target_pairs={{0,4},{4,8},{8,12},{12,0},{1,5},{5,9},{9,13},{13,1},{2,6},{6,10},{... | collective-permute-start | bytes 1572872 | tf_op jit(solution)/shard_map/kv_ring/ppermute | solution.py:151
  151.8 8.6 %collective-permute-start.16 = (bf16[2,512,256]{2,1,0:T(8,128)(2,1)S(1)}, bf16[2,512,256]{2,1,0:T(8,128)(2,1)S(1)}, u32[]{:S(2)}, u32[]{:S(2)}) collective-permute-start(bf16[2,512,256]{2,1,0:T(8,128)(2,1)S(1)} %collective-permute-done.15), channel_id=1, source_target_pairs={{0,4},{4,8},{8,12},{12,0},{1,5},{5,9},{9,13},{13,1},{2,6},{6,10},{... | collective-permute-start | bytes 1572872 | tf_op jit(solution)/shard_map/kv_ring/ppermute | solution.py:151
  167.5 10.6 %collective-permute-start.17 = (bf16[128,1536]{1,0:T(8,128)(2,1)S(1)}, bf16[128,1536]{1,0:T(8,128)(2,1)S(1)}, u32[]{:S(2)}, u32[]{:S(2)}) collective-permute-start(bf16[128,1536]{1,0:T(8,128)(2,1)S(1)} %get-tuple-element.16), channel_id=1, source_target_pairs={{0,1},{1,2},{2,3},{4,5},{5,6},{6,7},{8,9},{9,10},{10,11},{12,13},{... | collective-permute-start | bytes 1179656 | tf_op jit(solution)/shard_map/out_reduce/ppermute | solution.py:54
  169.8 12.9 %collective-permute-start.20 = (bf16[128,1536]{1,0:T(8,128)(2,1)S(1)}, bf16[128,1536]{1,0:T(8,128)(2,1)S(1)}, u32[]{:S(2)}, u32[]{:S(2)}) collective-permute-start(bf16[128,1536]{1,0:T(8,128)(2,1)S(1)} %get-tuple-element.17), channel_id=1, source_target_pairs={{1,0},{2,1},{3,2},{5,4},{6,5},{7,6},{9,8},{10,9},{11,10},{13,12},{... | collective-permute-start | bytes 1179656 | tf_op jit(solution)/shard_map/out_reduce/ppermute | solution.py:55
  178.2 11.7 %collective-permute-start.18 = (bf16[128,1536]{1,0:T(8,128)(2,1)S(1)}, bf16[128,1536]{1,0:T(8,128)(2,1)S(1)}, u32[]{:S(2)}, u32[]{:S(2)}) collective-permute-start(bf16[128,1536]{1,0:T(8,128)(2,1)S(1)} %fusion.58), channel_id=1, source_target_pairs={{0,1},{1,2},{2,3},{4,5},{5,6},{6,7},{8,9},{9,10},{10,11},{12,13},{... | collective-permute-start | bytes 1179656 | tf_op jit(solution)/shard_map/out_reduce/ppermute | solution.py:54
  190.1 12.0 %collective-permute-start.21 = (bf16[128,1536]{1,0:T(8,128)(2,1)S(1)}, bf16[128,1536]{1,0:T(8,128)(2,1)S(1)}, u32[]{:S(2)}, u32[]{:S(2)}) collective-permute-start(bf16[128,1536]{1,0:T(8,128)(2,1)S(1)} %get-tuple-element.15), channel_id=1, source_target_pairs={{1,0},{2,1},{3,2},{5,4},{6,5},{7,6},{9,8},{10,9},{11,10},{13,12},{... | collective-permute-start | bytes 1179656 | tf_op jit(solution)/shard_map/out_reduce/ppermute | solution.py:55
  191.6 12.1 %collective-permute-start.19 = (bf16[128,1536]{1,0:T(8,128)(2,1)S(1)}, bf16[128,1536]{1,0:T(8,128)(2,1)S(1)}, u32[]{:S(2)}, u32[]{:S(2)}) collective-permute-start(bf16[128,1536]{1,0:T(8,128)(2,1)S(1)} %get-tuple-element.14), channel_id=1, source_target_pairs={{0,1},{1,2},{2,3},{4,5},{5,6},{6,7},{8,9},{9,10},{10,11},{12,13},{... | collective-permute-start | bytes 1179656 | tf_op jit(solution)/shard_map/out_reduce/ppermute | solution.py:54
  202.2 9.8 %collective-permute-start.22 = (bf16[128,1536]{1,0:T(8,128)(2,1)S(1)}, bf16[128,1536]{1,0:T(8,128)(2,1)S(1)}, u32[]{:S(2)}, u32[]{:S(2)}) collective-permute-start(bf16[128,1536]{1,0:T(8,128)(2,1)S(1)} %fusion.57), channel_id=1, source_target_pairs={{1,0},{2,1},{3,2},{5,4},{6,5},{7,6},{9,8},{10,9},{11,10},{13,12},{... | collective-permute-start | bytes 1179656 | tf_op jit(solution)/shard_map/out_reduce/ppermute | solution.py:55
  (13 other events, 301.6 us)
where the time goes:
time: 229 us; the launch traced here: 228 us
  waiting for transfers between devices  125 us (55%)
  starting transfers between devices  62.1 us (27%)
  matrix products  15.6 us (7%)
  other arithmetic  13.1 us (6%)
  local copies, waits for them, and re-layouts  10.8 us (5%)
    ppermute x6, waiting for transfers between devices, line_reduce_scatter(): got_l = lax.ppermute(send_l, axis, left)  32.6 us
    ppermute x6, waiting for transfers between devices, line_reduce_scatter(): got_r = lax.ppermute(send_r, axis, right)  28.1 us
    ppermute x6, starting transfers between devices, line_reduce_scatter(): got_r = lax.ppermute(send_r, axis, right)  25 us
    ppermute x3, waiting for transfers between devices, shards(): arriving = lax.ppermute(current, 'seq', ring)  24.4 us
    ppermute x3, waiting for transfers between devices, line_all_gather(): flow_r = lax.ppermute(flow_r, axis, right)  13.1 us
    ppermute x3, starting transfers between devices, line_all_gather(): flow_r = lax.ppermute(flow_r, axis, right)  12.2 us
    all_to_all x1, waiting for transfers between devices, shards(): lax.all_to_all(normed, 'pair', split_axis=1, concat_axis=0, tiled=True)  11.7 us
    ppermute x4, waiting for transfers between devices, doubling_all_gather(): other = lax.ppermute(out, axis, [(i, i ^ k) for i in range(n)])  9.48 us
  transfers between devices with their start and end apart: 28, of which 21 were waited for; matrix products, arithmetic and copies ran while one was open for 5% of the time, Pallas kernels for 0%

commit v1 on v0

--- a/solution.py
+++ b/solution.py
@@ -100,7 +100,9 @@
     local_rows = row_count * pair_count
     inputs = sequence.astype(jnp.float32)
     normed = norm_rows(inputs, gain_conv).astype(jnp.bfloat16)
-    swapped = lax.all_to_all(normed, "pair", split_axis=1, concat_axis=0, tiled=True)
+    pieces = jnp.split(normed, lax.axis_size("pair"), axis=1)
+    arrived = lax.all_to_all(jnp.stack(pieces), "pair", 0, 0)
+    swapped = jnp.concatenate(arrived, axis=0)
     padded = padded_2(swapped, (("seq", 0),), DILATION * (conv_weight.shape[0] - 1) // 2)
     with jax.named_scope("conv_reduce"):
         summed = line_reduce_scatter(conv_rows(padded, conv_weight, local_rows), "pair")

time: 229 us -> 229 us (level)
  no operation moved by 1% of the time
where the time goes in v1:
time: 229 us; the launch traced here: 228 us
  waiting for transfers between devices  125 us (55%)
  starting transfers between devices  62.2 us (27%)
  matrix products  15.6 us (7%)
  other arithmetic  14 us (6%)
  local copies, waits for them, and re-layouts  10.2 us (4%)
    ppermute x6, waiting for transfers between devices, line_reduce_scatter(): got_l = lax.ppermute(send_l, axis, left)  32.6 us
    ppermute x6, waiting for transfers between devices, line_reduce_scatter(): got_r = lax.ppermute(send_r, axis, right)  28.1 us
    ppermute x6, starting transfers between devices, line_reduce_scatter(): got_r = lax.ppermute(send_r, axis, right)  25 us
    ppermute x3, waiting for transfers between devices, shards(): arriving = lax.ppermute(current, 'seq', ring)  24.4 us
    ppermute x3, waiting for transfers between devices, line_all_gather(): flow_r = lax.ppermute(flow_r, axis, right)  13.1 us
    ppermute x3, starting transfers between devices, line_all_gather(): flow_r = lax.ppermute(flow_r, axis, right)  12.2 us
    all_to_all x1, waiting for transfers between devices, shards(): arrived = lax.all_to_all(jnp.stack(pieces), 'pair', 0, 0)  11.7 us
    ppermute x4, waiting for transfers between devices, doubling_all_gather(): other = lax.ppermute(out, axis, [(i, i ^ k) for i in range(n)])  9.4 us
  transfers between devices with their start and end apart: 28, of which 21 were waited for; matrix products, arithmetic and copies ran while one was open for 5% of the time, Pallas kernels for 0%

profile of v1, /device:TPU:0, one launch (start us, length us, event | category | flops | bytes accessed | tf_op | source)
XLA Modules:
  0.0 228.2 jit_solution(12920656637107736659)
XLA Ops:
  4.0 6.3 %all-to-all-start = ((bf16[4,128,384]{2,1,0:T(8,128)(2,1)}), bf16[4,128,384]{2,1,0:T(8,128)(2,1)S(1)}, u32[]{:S(2)}, u32[]{:S(2)}) async-start(bf16[4,128,384]{2,1,0:T(8,128)(2,1)} %pad_maximum_fusion.4), calls=%async_computation | async-start | bytes 786432 | tf_op jit(solution)/shard_map/all_to_all | solution.py:104
  10.3 11.7 %all-to-all-done = bf16[4,128,384]{2,1,0:T(8,128)(2,1)S(1)} async-done(((bf16[4,128,384]{2,1,0:T(8,128)(2,1)}), bf16[4,128,384]{2,1,0:T(8,128)(2,1)S(1)}, u32[]{:S(2)}, u32[]{:S(2)}) %all-to-all-start) | async-done | bytes 393248 | tf_op jit(solution)/shard_map/all_to_all | solution.py:104
  38.8 5.8 %collective-permute-done.2 = bf16[128,1536]{1,0:T(8,128)(2,1)} collective-permute-done((bf16[128,1536]{1,0:T(8,128)(2,1)S(1)}, bf16[128,1536]{1,0:T(8,128)(2,1)}, u32[]{:S(2)}, u32[]{:S(2)}) %collective-permute-start.2) | collective-permute-done | bytes 393248 | tf_op jit(solution)/shard_map/conv_reduce/ppermute | solution.py:54
  45.9 5.2 %collective-permute-start.3 = (bf16[128,1536]{1,0:T(8,128)(2,1)S(1)}, bf16[128,1536]{1,0:T(8,128)(2,1)}, u32[]{:S(2)}, u32[]{:S(2)}) collective-permute-start(bf16[128,1536]{1,0:T(8,128)(2,1)S(1)} %fusion.65), channel_id=1, source_target_pairs={{0,1},{1,2},{2,3},{4,5},{5,6},{6,7},{8,9},{9,10},{10,11},{12,13},{... | collective-permute-start | bytes 1179656 | tf_op jit(solution)/shard_map/conv_reduce/ppermute | solution.py:54
  51.2 8.0 %collective-permute-done.3 = bf16[128,1536]{1,0:T(8,128)(2,1)} collective-permute-done((bf16[128,1536]{1,0:T(8,128)(2,1)S(1)}, bf16[128,1536]{1,0:T(8,128)(2,1)}, u32[]{:S(2)}, u32[]{:S(2)}) %collective-permute-start.3) | collective-permute-done | bytes 393248 | tf_op jit(solution)/shard_map/conv_reduce/ppermute | solution.py:54
  62.9 5.9 %collective-permute-start.4 = (bf16[128,1536]{1,0:T(8,128)(2,1)}, bf16[128,1536]{1,0:T(8,128)(2,1)}, u32[]{:S(2)}, u32[]{:S(2)}) collective-permute-start(bf16[128,1536]{1,0:T(8,128)(2,1)} %get-tuple-element.18), channel_id=1, source_target_pairs={{0,1},{1,2},{2,3},{4,5},{5,6},{6,7},{8,9},{9,10},{10,11},{12,13},{... | collective-permute-start | bytes 1179656 | tf_op jit(solution)/shard_map/conv_reduce/ppermute | solution.py:54
  68.9 7.1 %collective-permute-done.6 = bf16[128,1536]{1,0:T(8,128)(2,1)S(1)} collective-permute-done((bf16[128,1536]{1,0:T(8,128)(2,1)S(1)}, bf16[128,1536]{1,0:T(8,128)(2,1)S(1)}, u32[]{:S(2)}, u32[]{:S(2)}) %collective-permute-start.6) | collective-permute-done | bytes 393248 | tf_op jit(solution)/shard_map/conv_reduce/ppermute | solution.py:55
  78.5 11.6 %collective-permute-done.7 = bf16[128,1536]{1,0:T(8,128)(2,1)S(1)} collective-permute-done((bf16[128,1536]{1,0:T(8,128)(2,1)S(1)}, bf16[128,1536]{1,0:T(8,128)(2,1)S(1)}, u32[]{:S(2)}, u32[]{:S(2)}) %collective-permute-start.7) | collective-permute-done | bytes 393248 | tf_op jit(solution)/shard_map/conv_reduce/ppermute | solution.py:55
  94.2 3.6 %collective-permute-start.8 = (bf16[128,1536]{1,0:T(8,128)(2,1)}, bf16[128,1536]{1,0:T(8,128)(2,1)S(1)}, u32[]{:S(2)}, u32[]{:S(2)}) collective-permute-start(bf16[128,1536]{1,0:T(8,128)(2,1)} %get-tuple-element.11), channel_id=1, source_target_pairs={{0,1},{1,2},{2,3},{4,5},{5,6},{6,7},{8,9},{9,10},{10,11},{12,13},{... | collective-permute-start | bytes 1179656 | tf_op jit(solution)/shard_map/attn_in_gather/ppermute | solution.py:70
  99.1 6.5 %collective-permute-done.8 = bf16[128,1536]{1,0:T(8,128)(2,1)S(1)} collective-permute-done((bf16[128,1536]{1,0:T(8,128)(2,1)}, bf16[128,1536]{1,0:T(8,128)(2,1)S(1)}, u32[]{:S(2)}, u32[]{:S(2)}) %collective-permute-start.8) | collective-permute-done | bytes 393248 | tf_op jit(solution)/shard_map/attn_in_gather/ppermute | solution.py:70
  105.6 4.3 %collective-permute-start.10 = (bf16[128,1536]{1,0:T(8,128)(2,1)S(1)}, bf16[128,1536]{1,0:T(8,128)(2,1)S(1)}, u32[]{:S(2)}, u32[]{:S(2)}) collective-permute-start(bf16[128,1536]{1,0:T(8,128)(2,1)S(1)} %collective-permute-done.8), channel_id=1, source_target_pairs={{0,1},{1,2},{2,3},{4,5},{5,6},{6,7},{8,9},{9,10},{10,11},{12,13},{... | collective-permute-start | bytes 1179656 | tf_op jit(solution)/shard_map/attn_in_gather/ppermute | solution.py:70
  112.8 3.8 %collective-permute-done.10 = bf16[128,1536]{1,0:T(8,128)(2,1)S(1)} collective-permute-done((bf16[128,1536]{1,0:T(8,128)(2,1)S(1)}, bf16[128,1536]{1,0:T(8,128)(2,1)S(1)}, u32[]{:S(2)}, u32[]{:S(2)}) %collective-permute-start.10) | collective-permute-done | bytes 393248 | tf_op jit(solution)/shard_map/attn_in_gather/ppermute | solution.py:70
  116.6 4.4 %collective-permute-start.12 = (bf16[128,1536]{1,0:T(8,128)(2,1)S(1)}, bf16[128,1536]{1,0:T(8,128)(2,1)S(1)}, u32[]{:S(2)}, u32[]{:S(2)}) collective-permute-start(bf16[128,1536]{1,0:T(8,128)(2,1)S(1)} %collective-permute-done.10), channel_id=1, source_target_pairs={{0,1},{1,2},{2,3},{4,5},{5,6},{6,7},{8,9},{9,10},{10,11},{12,13},{... | collective-permute-start | bytes 1179656 | tf_op jit(solution)/shard_map/attn_in_gather/ppermute | solution.py:70
  127.5 3.4 %collective-permute-done.13 = bf16[128,1536]{1,0:T(8,128)(2,1)S(1)} collective-permute-done((bf16[128,1536]{1,0:T(8,128)(2,1)S(1)}, bf16[128,1536]{1,0:T(8,128)(2,1)S(1)}, u32[]{:S(2)}, u32[]{:S(2)}) %collective-permute-start.13) | collective-permute-done | bytes 393248 | tf_op jit(solution)/shard_map/attn_in_gather/ppermute | solution.py:71
  134.7 8.6 %collective-permute-done.14 = bf16[2,512,256]{2,1,0:T(8,128)(2,1)S(1)} collective-permute-done((bf16[2,512,256]{2,1,0:T(8,128)(2,1)S(1)}, bf16[2,512,256]{2,1,0:T(8,128)(2,1)S(1)}, u32[]{:S(2)}, u32[]{:S(2)}) %collective-permute-start.14) | collective-permute-done | bytes 524320 | tf_op jit(solution)/shard_map/kv_ring/ppermute | solution.py:153
  143.8 8.2 %collective-permute-done.15 = bf16[2,512,256]{2,1,0:T(8,128)(2,1)S(1)} collective-permute-done((bf16[2,512,256]{2,1,0:T(8,128)(2,1)S(1)}, bf16[2,512,256]{2,1,0:T(8,128)(2,1)S(1)}, u32[]{:S(2)}, u32[]{:S(2)}) %collective-permute-start.15) | collective-permute-done | bytes 524320 | tf_op jit(solution)/shard_map/kv_ring/ppermute | solution.py:153
  152.8 7.7 %collective-permute-done.16 = bf16[2,512,256]{2,1,0:T(8,128)(2,1)S(1)} collective-permute-done((bf16[2,512,256]{2,1,0:T(8,128)(2,1)S(1)}, bf16[2,512,256]{2,1,0:T(8,128)(2,1)S(1)}, u32[]{:S(2)}, u32[]{:S(2)}) %collective-permute-start.16) | collective-permute-done | bytes 524320 | tf_op jit(solution)/shard_map/kv_ring/ppermute | solution.py:153
  171.2 7.1 %collective-permute-done.17 = bf16[128,1536]{1,0:T(8,128)(2,1)S(1)} collective-permute-done((bf16[128,1536]{1,0:T(8,128)(2,1)S(1)}, bf16[128,1536]{1,0:T(8,128)(2,1)S(1)}, u32[]{:S(2)}, u32[]{:S(2)}) %collective-permute-start.17) | collective-permute-done | bytes 393248 | tf_op jit(solution)/shard_map/out_reduce/ppermute | solution.py:54
  178.4 4.4 %collective-permute-start.18 = (bf16[128,1536]{1,0:T(8,128)(2,1)S(1)}, bf16[128,1536]{1,0:T(8,128)(2,1)S(1)}, u32[]{:S(2)}, u32[]{:S(2)}) collective-permute-start(bf16[128,1536]{1,0:T(8,128)(2,1)S(1)} %fusion.58), channel_id=1, source_target_pairs={{0,1},{1,2},{2,3},{4,5},{5,6},{6,7},{8,9},{9,10},{10,11},{12,13},{... | collective-permute-start | bytes 1179656 | tf_op jit(solution)/shard_map/out_reduce/ppermute | solution.py:54
  182.8 7.3 %collective-permute-done.18 = bf16[128,1536]{1,0:T(8,128)(2,1)S(1)} collective-permute-done((bf16[128,1536]{1,0:T(8,128)(2,1)S(1)}, bf16[128,1536]{1,0:T(8,128)(2,1)S(1)}, u32[]{:S(2)}, u32[]{:S(2)}) %collective-permute-start.18) | collective-permute-done | bytes 393248 | tf_op jit(solution)/shard_map/out_reduce/ppermute | solution.py:54
  191.7 5.0 %collective-permute-start.19 = (bf16[128,1536]{1,0:T(8,128)(2,1)S(1)}, bf16[128,1536]{1,0:T(8,128)(2,1)S(1)}, u32[]{:S(2)}, u32[]{:S(2)}) collective-permute-start(bf16[128,1536]{1,0:T(8,128)(2,1)S(1)} %get-tuple-element.14), channel_id=1, source_target_pairs={{0,1},{1,2},{2,3},{4,5},{5,6},{6,7},{8,9},{9,10},{10,11},{12,13},{... | collective-permute-start | bytes 1179656 | tf_op jit(solution)/shard_map/out_reduce/ppermute | solution.py:54
  196.7 5.5 %collective-permute-done.21 = bf16[128,1536]{1,0:T(8,128)(2,1)S(1)} collective-permute-done((bf16[128,1536]{1,0:T(8,128)(2,1)S(1)}, bf16[128,1536]{1,0:T(8,128)(2,1)S(1)}, u32[]{:S(2)}, u32[]{:S(2)}) %collective-permute-start.21) | collective-permute-done | bytes 393248 | tf_op jit(solution)/shard_map/out_reduce/ppermute | solution.py:55
  203.8 8.4 %collective-permute-done.22 = bf16[128,1536]{1,0:T(8,128)(2,1)S(1)} collective-permute-done((bf16[128,1536]{1,0:T(8,128)(2,1)S(1)}, bf16[128,1536]{1,0:T(8,128)(2,1)S(1)}, u32[]{:S(2)}, u32[]{:S(2)}) %collective-permute-start.22) | collective-permute-done | bytes 393248 | tf_op jit(solution)/shard_map/out_reduce/ppermute | solution.py:55
  223.1 3.8 %collective-permute-done.26 = bf16[64,256]{1,0:T(8,128)(2,1)S(1)} collective-permute-done((bf16[64,256]{1,0:T(8,128)(2,1)S(1)}, bf16[64,256]{1,0:T(8,128)(2,1)S(1)}, u32[]{:S(2)}, u32[]{:S(2)}) %collective-permute-start.26) | collective-permute-done | bytes 32800 | tf_op jit(solution)/shard_map/sides_gather/ppermute | solution.py:86
  (109 shorter events, 73.6 us)
Async XLA Ops:
  4.0 18.0 %all-to-all-start = ((bf16[4,128,384]{2,1,0:T(8,128)(2,1)}), bf16[4,128,384]{2,1,0:T(8,128)(2,1)S(1)}, u32[]{:S(2)}, u32[]{:S(2)}) async-start(bf16[4,128,384]{2,1,0:T(8,128)(2,1)} %pad_maximum_fusion.4), calls=%async_computation | async-start | bytes 786432 | tf_op jit(solution)/shard_map/all_to_all | solution.py:104
  22.0 5.3 %collective-permute-start = (bf16[8,384]{1,0:T(8,128)(2,1)S(1)}, bf16[8,384]{1,0:T(8,128)(2,1)S(1)}, u32[]{:S(2)}, u32[]{:S(2)}) collective-permute-start(bf16[8,384]{1,0:T(8,128)(2,1)S(1)} %get-tuple-element.22), channel_id=1, source_target_pairs={{0,4},{4,8},{8,12},{1,5},{5,9},{9,13},{2,6},{6,10},{10,14},{3,7},{... | collective-permute-start | bytes 18440 | tf_op jit(solution)/shard_map/ppermute | solution.py:22
  26.0 4.7 %collective-permute-start.1 = (bf16[8,384]{1,0:T(8,128)(2,1)S(1)}, bf16[8,384]{1,0:T(8,128)(2,1)S(1)}, u32[]{:S(2)}, u32[]{:S(2)}) collective-permute-start(bf16[8,384]{1,0:T(8,128)(2,1)S(1)} %get-tuple-element.23), channel_id=1, source_target_pairs={{4,0},{8,4},{12,8},{5,1},{9,5},{13,9},{6,2},{10,6},{14,10},{7,3},{... | collective-permute-start | bytes 18440 | tf_op jit(solution)/shard_map/ppermute | solution.py:23
  35.3 9.3 %collective-permute-start.2 = (bf16[128,1536]{1,0:T(8,128)(2,1)S(1)}, bf16[128,1536]{1,0:T(8,128)(2,1)}, u32[]{:S(2)}, u32[]{:S(2)}) collective-permute-start(bf16[128,1536]{1,0:T(8,128)(2,1)S(1)} %get-tuple-element.20), channel_id=1, source_target_pairs={{0,1},{1,2},{2,3},{4,5},{5,6},{6,7},{8,9},{9,10},{10,11},{12,13},{... | collective-permute-start | bytes 1179656 | tf_op jit(solution)/shard_map/conv_reduce/ppermute | solution.py:54
  37.5 13.7 %collective-permute-start.5 = (bf16[128,1536]{1,0:T(8,128)(2,1)S(1)}, bf16[128,1536]{1,0:T(8,128)(2,1)}, u32[]{:S(2)}, u32[]{:S(2)}) collective-permute-start(bf16[128,1536]{1,0:T(8,128)(2,1)S(1)} %get-tuple-element.21), channel_id=1, source_target_pairs={{1,0},{2,1},{3,2},{5,4},{6,5},{7,6},{9,8},{10,9},{11,10},{13,12},{... | collective-permute-start | bytes 1179656 | tf_op jit(solution)/shard_map/conv_reduce/ppermute | solution.py:55
  45.9 13.2 %collective-permute-start.3 = (bf16[128,1536]{1,0:T(8,128)(2,1)S(1)}, bf16[128,1536]{1,0:T(8,128)(2,1)}, u32[]{:S(2)}, u32[]{:S(2)}) collective-permute-start(bf16[128,1536]{1,0:T(8,128)(2,1)S(1)} %fusion.65), channel_id=1, source_target_pairs={{0,1},{1,2},{2,3},{4,5},{5,6},{6,7},{8,9},{9,10},{10,11},{12,13},{... | collective-permute-start | bytes 1179656 | tf_op jit(solution)/shard_map/conv_reduce/ppermute | solution.py:54
  61.7 14.3 %collective-permute-start.6 = (bf16[128,1536]{1,0:T(8,128)(2,1)S(1)}, bf16[128,1536]{1,0:T(8,128)(2,1)S(1)}, u32[]{:S(2)}, u32[]{:S(2)}) collective-permute-start(bf16[128,1536]{1,0:T(8,128)(2,1)S(1)} %get-tuple-element.19), channel_id=1, source_target_pairs={{1,0},{2,1},{3,2},{5,4},{6,5},{7,6},{9,8},{10,9},{11,10},{13,12},{... | collective-permute-start | bytes 1179656 | tf_op jit(solution)/shard_map/conv_reduce/ppermute | solution.py:55
  62.9 15.6 %collective-permute-start.4 = (bf16[128,1536]{1,0:T(8,128)(2,1)}, bf16[128,1536]{1,0:T(8,128)(2,1)}, u32[]{:S(2)}, u32[]{:S(2)}) collective-permute-start(bf16[128,1536]{1,0:T(8,128)(2,1)} %get-tuple-element.18), channel_id=1, source_target_pairs={{0,1},{1,2},{2,3},{4,5},{5,6},{6,7},{8,9},{9,10},{10,11},{12,13},{... | collective-permute-start | bytes 1179656 | tf_op jit(solution)/shard_map/conv_reduce/ppermute | solution.py:54
  77.2 12.9 %collective-permute-start.7 = (bf16[128,1536]{1,0:T(8,128)(2,1)S(1)}, bf16[128,1536]{1,0:T(8,128)(2,1)S(1)}, u32[]{:S(2)}, u32[]{:S(2)}) collective-permute-start(bf16[128,1536]{1,0:T(8,128)(2,1)S(1)} %fusion.64), channel_id=1, source_target_pairs={{1,0},{2,1},{3,2},{5,4},{6,5},{7,6},{9,8},{10,9},{11,10},{13,12},{... | collective-permute-start | bytes 1179656 | tf_op jit(solution)/shard_map/conv_reduce/ppermute | solution.py:55
  94.2 11.4 %collective-permute-start.8 = (bf16[128,1536]{1,0:T(8,128)(2,1)}, bf16[128,1536]{1,0:T(8,128)(2,1)S(1)}, u32[]{:S(2)}, u32[]{:S(2)}) collective-permute-start(bf16[128,1536]{1,0:T(8,128)(2,1)} %get-tuple-element.11), channel_id=1, source_target_pairs={{0,1},{1,2},{2,3},{4,5},{5,6},{6,7},{8,9},{9,10},{10,11},{12,13},{... | collective-permute-start | bytes 1179656 | tf_op jit(solution)/shard_map/attn_in_gather/ppermute | solution.py:70
  97.8 12.2 %collective-permute-start.9 = (bf16[128,1536]{1,0:T(8,128)(2,1)}, bf16[128,1536]{1,0:T(8,128)(2,1)S(1)}, u32[]{:S(2)}, u32[]{:S(2)}) collective-permute-start(bf16[128,1536]{1,0:T(8,128)(2,1)} %get-tuple-element.11), channel_id=1, source_target_pairs={{1,0},{2,1},{3,2},{5,4},{6,5},{7,6},{9,8},{10,9},{11,10},{13,12},{... | collective-permute-start | bytes 1179656 | tf_op jit(solution)/shard_map/attn_in_gather/ppermute | solution.py:71
  105.6 10.9 %collective-permute-start.10 = (bf16[128,1536]{1,0:T(8,128)(2,1)S(1)}, bf16[128,1536]{1,0:T(8,128)(2,1)S(1)}, u32[]{:S(2)}, u32[]{:S(2)}) collective-permute-start(bf16[128,1536]{1,0:T(8,128)(2,1)S(1)} %collective-permute-done.8), channel_id=1, source_target_pairs={{0,1},{1,2},{2,3},{4,5},{5,6},{6,7},{8,9},{9,10},{10,11},{12,13},{... | collective-permute-start | bytes 1179656 | tf_op jit(solution)/shard_map/attn_in_gather/ppermute | solution.py:70
  110.0 11.0 %collective-permute-start.11 = (bf16[128,1536]{1,0:T(8,128)(2,1)S(1)}, bf16[128,1536]{1,0:T(8,128)(2,1)S(1)}, u32[]{:S(2)}, u32[]{:S(2)}) collective-permute-start(bf16[128,1536]{1,0:T(8,128)(2,1)S(1)} %collective-permute-done.9), channel_id=1, source_target_pairs={{1,0},{2,1},{3,2},{5,4},{6,5},{7,6},{9,8},{10,9},{11,10},{13,12},{... | collective-permute-start | bytes 1179656 | tf_op jit(solution)/shard_map/attn_in_gather/ppermute | solution.py:71
  116.6 10.1 %collective-permute-start.12 = (bf16[128,1536]{1,0:T(8,128)(2,1)S(1)}, bf16[128,1536]{1,0:T(8,128)(2,1)S(1)}, u32[]{:S(2)}, u32[]{:S(2)}) collective-permute-start(bf16[128,1536]{1,0:T(8,128)(2,1)S(1)} %collective-permute-done.10), channel_id=1, source_target_pairs={{0,1},{1,2},{2,3},{4,5},{5,6},{6,7},{8,9},{9,10},{10,11},{12,13},{... | collective-permute-start | bytes 1179656 | tf_op jit(solution)/shard_map/attn_in_gather/ppermute | solution.py:70
  121.0 9.9 %collective-permute-start.13 = (bf16[128,1536]{1,0:T(8,128)(2,1)S(1)}, bf16[128,1536]{1,0:T(8,128)(2,1)S(1)}, u32[]{:S(2)}, u32[]{:S(2)}) collective-permute-start(bf16[128,1536]{1,0:T(8,128)(2,1)S(1)} %collective-permute-done.11), channel_id=1, source_target_pairs={{1,0},{2,1},{3,2},{5,4},{6,5},{7,6},{9,8},{10,9},{11,10},{13,12},{... | collective-permute-start | bytes 1179656 | tf_op jit(solution)/shard_map/attn_in_gather/ppermute | solution.py:71
  134.7 8.7 %collective-permute-start.14 = (bf16[2,512,256]{2,1,0:T(8,128)(2,1)S(1)}, bf16[2,512,256]{2,1,0:T(8,128)(2,1)S(1)}, u32[]{:S(2)}, u32[]{:S(2)}) collective-permute-start(bf16[2,512,256]{2,1,0:T(8,128)(2,1)S(1)} %slice.92), channel_id=1, source_target_pairs={{0,4},{4,8},{8,12},{12,0},{1,5},{5,9},{9,13},{13,1},{2,6},{6,10},{... | collective-permute-start | bytes 1572872 | tf_op jit(solution)/shard_map/kv_ring/ppermute | solution.py:153
  143.3 8.6 %collective-permute-start.15 = (bf16[2,512,256]{2,1,0:T(8,128)(2,1)S(1)}, bf16[2,512,256]{2,1,0:T(8,128)(2,1)S(1)}, u32[]{:S(2)}, u32[]{:S(2)}) collective-permute-start(bf16[2,512,256]{2,1,0:T(8,128)(2,1)S(1)} %collective-permute-done.14), channel_id=1, source_target_pairs={{0,4},{4,8},{8,12},{12,0},{1,5},{5,9},{9,13},{13,1},{2,6},{6,10},{... | collective-permute-start | bytes 1572872 | tf_op jit(solution)/shard_map/kv_ring/ppermute | solution.py:153
  151.9 8.6 %collective-permute-start.16 = (bf16[2,512,256]{2,1,0:T(8,128)(2,1)S(1)}, bf16[2,512,256]{2,1,0:T(8,128)(2,1)S(1)}, u32[]{:S(2)}, u32[]{:S(2)}) collective-permute-start(bf16[2,512,256]{2,1,0:T(8,128)(2,1)S(1)} %collective-permute-done.15), channel_id=1, source_target_pairs={{0,4},{4,8},{8,12},{12,0},{1,5},{5,9},{9,13},{13,1},{2,6},{6,10},{... | collective-permute-start | bytes 1572872 | tf_op jit(solution)/shard_map/kv_ring/ppermute | solution.py:153
  167.6 10.6 %collective-permute-start.17 = (bf16[128,1536]{1,0:T(8,128)(2,1)S(1)}, bf16[128,1536]{1,0:T(8,128)(2,1)S(1)}, u32[]{:S(2)}, u32[]{:S(2)}) collective-permute-start(bf16[128,1536]{1,0:T(8,128)(2,1)S(1)} %get-tuple-element.16), channel_id=1, source_target_pairs={{0,1},{1,2},{2,3},{4,5},{5,6},{6,7},{8,9},{9,10},{10,11},{12,13},{... | collective-permute-start | bytes 1179656 | tf_op jit(solution)/shard_map/out_reduce/ppermute | solution.py:54
  169.9 12.9 %collective-permute-start.20 = (bf16[128,1536]{1,0:T(8,128)(2,1)S(1)}, bf16[128,1536]{1,0:T(8,128)(2,1)S(1)}, u32[]{:S(2)}, u32[]{:S(2)}) collective-permute-start(bf16[128,1536]{1,0:T(8,128)(2,1)S(1)} %get-tuple-element.17), channel_id=1, source_target_pairs={{1,0},{2,1},{3,2},{5,4},{6,5},{7,6},{9,8},{10,9},{11,10},{13,12},{... | collective-permute-start | bytes 1179656 | tf_op jit(solution)/shard_map/out_reduce/ppermute | solution.py:55
  178.4 11.7 %collective-permute-start.18 = (bf16[128,1536]{1,0:T(8,128)(2,1)S(1)}, bf16[128,1536]{1,0:T(8,128)(2,1)S(1)}, u32[]{:S(2)}, u32[]{:S(2)}) collective-permute-start(bf16[128,1536]{1,0:T(8,128)(2,1)S(1)} %fusion.58), channel_id=1, source_target_pairs={{0,1},{1,2},{2,3},{4,5},{5,6},{6,7},{8,9},{9,10},{10,11},{12,13},{... | collective-permute-start | bytes 1179656 | tf_op jit(solution)/shard_map/out_reduce/ppermute | solution.py:54
  190.3 12.0 %collective-permute-start.21 = (bf16[128,1536]{1,0:T(8,128)(2,1)S(1)}, bf16[128,1536]{1,0:T(8,128)(2,1)S(1)}, u32[]{:S(2)}, u32[]{:S(2)}) collective-permute-start(bf16[128,1536]{1,0:T(8,128)(2,1)S(1)} %get-tuple-element.15), channel_id=1, source_target_pairs={{1,0},{2,1},{3,2},{5,4},{6,5},{7,6},{9,8},{10,9},{11,10},{13,12},{... | collective-permute-start | bytes 1179656 | tf_op jit(solution)/shard_map/out_reduce/ppermute | solution.py:55
  191.7 12.1 %collective-permute-start.19 = (bf16[128,1536]{1,0:T(8,128)(2,1)S(1)}, bf16[128,1536]{1,0:T(8,128)(2,1)S(1)}, u32[]{:S(2)}, u32[]{:S(2)}) collective-permute-start(bf16[128,1536]{1,0:T(8,128)(2,1)S(1)} %get-tuple-element.14), channel_id=1, source_target_pairs={{0,1},{1,2},{2,3},{4,5},{5,6},{6,7},{8,9},{9,10},{10,11},{12,13},{... | collective-permute-start | bytes 1179656 | tf_op jit(solution)/shard_map/out_reduce/ppermute | solution.py:54
  202.4 9.8 %collective-permute-start.22 = (bf16[128,1536]{1,0:T(8,128)(2,1)S(1)}, bf16[128,1536]{1,0:T(8,128)(2,1)S(1)}, u32[]{:S(2)}, u32[]{:S(2)}) collective-permute-start(bf16[128,1536]{1,0:T(8,128)(2,1)S(1)} %fusion.57), channel_id=1, source_target_pairs={{1,0},{2,1},{3,2},{5,4},{6,5},{7,6},{9,8},{10,9},{11,10},{13,12},{... | collective-permute-start | bytes 1179656 | tf_op jit(solution)/shard_map/out_reduce/ppermute | solution.py:55
  (13 other events, 301.7 us)
